TPU v7x, 128 devices: a whole 4x4x4 slice. The times are simulated.
128 devices in a mesh: row: 8 (over x, y_hi), col: 16 (over y_lo, z, core).
Axes of the slice: x: 4, y: 4 (y_hi: 2, y_lo: 2; y = y_hi * 2 + y_lo), z: 4, core: 2. Of those that a mesh axis runs over, the one named last changes fastest.
Arguments:
- flat_gradient: bfloat16 [8, 16, 524288], P('row', 'col'), may hold values from -6 to 6
- range_rows: int32 [8, 16], replicated, may hold values from 1 to 64, 512 in all within a row
- left_stat: float32 [4096, 4096], P('row', 'col'), may hold values from -6 to 6
- right_stat: float32 [8192, 8192], P('col', 'row'), may hold values from -6 to 6
- left_root: bfloat16 [4096, 4096], P('row'), as said below
- right_root: bfloat16 [8192, 8192], P('col'), as said below
Outputs:
- left_new: float32 [4096, 4096], P('row', 'col')
- right_new: float32 [8192, 8192], P('col', 'row')
- update: bfloat16 [4096, 8192], P('row', 'col')
Inputs may be any that keep to these rules, and one draw needn't show every extreme that they name: In each row r the entries sum to 512; the largest entry of every row is exactly 64. Slots of flat_gradient beyond a device's range_rows rows are padding. left_root equals its transpose. right_root equals its transpose.
All inputs are finite; a program needn't handle non-finite values.
Results may differ from a plain program's by a relative error of at most 0.014.
Values may be sent and summed in bfloat16 or wider, within the bound.
No kernel may reach another device: no remote copies, remote signals or barrier semaphores. Data moves between devices by JAX's collectives and lax.ppermute only.
A program may use at most 192 MiB of HBM per device.

v0:
```python
import math
import jax
import jax.numpy as jnp
from jax import lax
from jax.sharding import PartitionSpec as P

HQ = 4096
DIN = 8192
stat_decay = 0.9


def shifted(block, axis, distance):
    devices = range(lax.axis_size(axis))
    route = [((i - distance) % len(devices), i) for i in devices]
    return lax.ppermute(block, axis, route)


def broadcast(block, axis, source):
    block = jnp.where(lax.axis_index(axis) == source, block, jnp.zeros_like(block))
    return lax.psum(block, axis)


def slot_index(row_counts, tile_rows, capacity):
    offsets = jnp.cumsum(row_counts) - row_counts
    target = jnp.arange(tile_rows, dtype=jnp.int32)
    covered = target[:, None] >= offsets[None, :]
    source = jnp.sum(covered.astype(jnp.int32), axis=1) - 1
    begins = jnp.max(jnp.where(covered, offsets[None, :], 0), axis=1)
    return source * capacity + target - begins


def shards(flat_gradient, range_rows, left_stat, right_stat, left_root, right_root):
    row_count = lax.axis_size("row")
    col_count = lax.axis_size("col")
    row_index = lax.axis_index("row")
    tile_rows = HQ // row_count
    capacity = flat_gradient.shape[2] // DIN
    held_rows = flat_gradient.reshape(capacity, DIN)
    received = lax.all_to_all(held_rows, "col", split_axis=1, concat_axis=0, tiled=True)
    row_counts = lax.dynamic_index_in_dim(range_rows, row_index, 0, keepdims=False)
    grad_tile = jnp.take(received, slot_index(row_counts, tile_rows, capacity), axis=0)
    column_panel = lax.all_gather(grad_tile, "row", axis=0, tiled=True)
    half_count = row_count // 2
    rotated = jnp.roll(column_panel, -row_index * tile_rows, axis=0)
    upper_part = lax.dot_general(
        grad_tile,
        rotated[: (half_count + 1) * tile_rows],
        (((1,), (1,)), ((), ())),
        preferred_element_type=jnp.float32,
    )
    upper_blocks = [
        upper_part[:, stride * tile_rows : (stride + 1) * tile_rows]
        for stride in range(half_count + 1)
    ]
    mirrored = {}
    for stride in range(1, half_count):
        mirrored[stride] = shifted(
            upper_blocks[stride].T.astype(jnp.bfloat16), "row", stride
        ).astype(jnp.float32)
    all_blocks = upper_blocks + [
        mirrored[row_count - distance] for distance in range(half_count + 1, row_count)
    ]
    left_part = jnp.roll(jnp.concatenate(all_blocks, axis=1), row_index * tile_rows, axis=1)
    left_sum = lax.psum_scatter(
        left_part.astype(jnp.bfloat16), "col", scatter_dimension=1, tiled=True
    ).astype(jnp.float32)
    panel_ratio = col_count // row_count
    partner_list = []
    for member in range(panel_ratio):
        partner_list.append(broadcast(column_panel, "col", row_index * panel_ratio + member))
    partner_panel = jnp.concatenate(partner_list, axis=1)
    right_gram = lax.dot_general(
        column_panel, partner_panel, (((0,), (0,)), ((), ())), preferred_element_type=jnp.float32
    )
    right_new = stat_decay * right_stat + right_gram * (1.0 / math.sqrt(HQ))
    left_mixed = jnp.dot(left_root, column_panel, preferred_element_type=jnp.float32).astype(
        jnp.bfloat16
    )
    update_sum = lax.dot_general(
        lax.all_gather(left_mixed, "col", axis=1, tiled=True),
        right_root,
        (((1,), (1,)), ((), ())),
        preferred_element_type=jnp.float32,
    )
    left_new = stat_decay * left_stat + left_sum * (1.0 / math.sqrt(DIN))
    return (left_new, right_new, update_sum.astype(jnp.bfloat16))


def solution(mesh):
    in_specs = (
        P("row", "col", None),
        P(),
        P("row", "col"),
        P("col", "row"),
        P("row", None),
        P("col", None),
    )
    out_specs = (P("row", "col"), P("col", "row"), P("row", "col"))
    return jax.shard_map(shards, mesh=mesh, in_specs=in_specs, out_specs=out_specs, check_vma=False)
```

profile of v0, /device:TPU:1, one launch (start us, length us, event | category | flops | bytes accessed | tf_op | source)
XLA Modules:
  0.0 440.1 jit_solution(12549819292666009770)
XLA Ops:
  7.2 22.8 %reduce = bf16[524288]{0:T(1024)(128)(2,1)S(1)} reduce(bf16[1,1,524288]{2,1,0:T(2,128)(2,1)} %param.6, bf16[]{:T(256)} %constant.91), dimensions={0,1}, to_apply=%param.6.reduce_sub_computation | reduce | bytes 2097154 | tf_op args[0]
  32.2 7.8 %all-to-all-start = ((bf16[64,16,512]{2,0,1:T(8,128)(2,1)}), bf16[64,16,512]{2,0,1:T(8,128)(2,1)S(1)}, u32[]{:S(2)}, u32[]{:S(2)}) async-start(bf16[64,16,512]{2,0,1:T(8,128)(2,1)} %copy.13), calls=%async_computation | async-start | bytes 2097152 | tf_op jit(solution)/shard_map/all_to_all | solution.py:39
  41.8 14.0 %all-to-all-done = bf16[64,16,512]{2,0,1:T(8,128)(2,1)S(1)} async-done(((bf16[64,16,512]{2,0,1:T(8,128)(2,1)}), bf16[64,16,512]{2,0,1:T(8,128)(2,1)S(1)}, u32[]{:S(2)}, u32[]{:S(2)}) %all-to-all-start) | async-done | bytes 1048608 | tf_op jit(solution)/shard_map/all_to_all | solution.py:39
  55.9 2.0 gather_fusion
  58.8 70.9 %all-gather.3.cloned.1.call-done = bf16[4096,512]{1,0:T(8,128)(2,1)} async-done(((bf16[512,512]{1,0:T(8,128)(2,1)}), bf16[4096,512]{1,0:T(8,128)(2,1)}) %all-gather.3.cloned.1.call-update) | async-done | bytes 4194320 | tf_op jit(solution)/shard_map/all_gather | solution.py:42
  129.7 6.0 %broadcast_select_fusion.1 = (bf16[4096,512]{1,0:T(8,128)(2,1)}, bf16[4096,512]{1,0:T(8,128)(2,1)}) fusion(bf16[4096,512]{1,0:T(8,128)(2,1)} %all-gather.3.cloned.1.call-done, pred[]{:T(512)S(6)} %eq.11, pred[]{:T(512)S(6)} %eq.12), kind=kLoop, calls=%fused_computation.9 | loop fusion | flops 4194304 | bytes 12582914 | tf_op jit(solution)/shard_map/jit(_where)/select_n | solution.py:19
  136.8 5.1 %constant_dynamic-update-slice_fusion.1 = (bf16[512,8192]{1,0:T(8,128)(2,1)}, bf16[512,2560]{1,0:T(8,128)(2,1)S(1)}) fusion(bf16[512,512]{1,0:T(8,128)(2,1)S(1)} %copy-done, s32[]{:T(128)S(6)} %select_n.71, bf16[4096,512]{1,0:T(8,128)(2,1)} %all-gather.3.cloned.1.call-done), kind=kOutput, calls=%fused_computation.31 | convolution fusion | flops 1347420160 | bytes 9961476 | tf_op jit(solution)/shard_map/dot_general | solution.py:45
  141.9 2.7 copy.14
  144.6 2.5 slice_bitcast_fusion
  147.9 3.2 collective-permute-start.2
  151.1 12.5 %collective-permute-done = bf16[512,512]{1,0:T(8,128)(2,1)S(1)} collective-permute-done((bf16[512,512]{1,0:T(8,128)(2,1)}, bf16[512,512]{1,0:T(8,128)(2,1)S(1)}, u32[]{:S(2)}, u32[]{:S(2)}) %collective-permute-start) | collective-permute-done | bytes 524320 | tf_op jit(solution)/shard_map/ppermute | solution.py:15
  164.5 7.7 %collective-permute-done.1 = bf16[512,512]{1,0:T(8,128)(2,1)} collective-permute-done((bf16[512,512]{1,0:T(8,128)(2,1)}, bf16[512,512]{1,0:T(8,128)(2,1)}, u32[]{:S(2)}, u32[]{:S(2)}) %collective-permute-start.1) | collective-permute-done | bytes 524320 | tf_op jit(solution)/shard_map/ppermute | solution.py:15
  172.2 1.9 convert_dynamic-update-slice_fusion.2
  174.1 13.5 %collective-permute-done.2 = bf16[512,512]{1,0:T(8,128)(2,1)S(1)} collective-permute-done((bf16[512,512]{1,0:T(8,128)(2,1)}, bf16[512,512]{1,0:T(8,128)(2,1)S(1)}, u32[]{:S(2)}, u32[]{:S(2)}) %collective-permute-start.2) | collective-permute-done | bytes 524320 | tf_op jit(solution)/shard_map/ppermute | solution.py:15
  188.4 1.7 constant_dynamic-update-slice_fusion
  191.0 2.0 convert_dynamic-update-slice_fusion.3
  193.9 4.7 %dynamic-slice_convert_fusion = bf16[512,4096]{1,0:T(8,128)(2,1)} fusion(bf16[512,8192]{1,0:T(8,128)(2,1)} %convert_dynamic-update-slice_fusion.1, s32[]{:T(128)S(6)} %select_n.73), kind=kLoop, calls=%fused_computation.7 | loop fusion | bytes 8388612 | tf_op jit(solution)/shard_map/convert_element_type | solution.py:65
  198.6 6.9 %fusion.9 = bf16[512,512]{0,1:T(8,128)(2,1)} fusion(bf16[4096,512]{1,0:T(8,128)(2,1)} %all-gather.3.cloned.1.call-done, bf16[512,4096]{1,0:T(8,128)(2,1)} %param.10), kind=kOutput, calls=%fused_computation.21 | convolution fusion | flops 2147745792 | bytes 8912896 | tf_op jit(solution)/shard_map/dot_general | solution.py:76
  205.5 92.8 %all-reduce.3.cloned.1.call-done = (bf16[4096,512]{1,0:T(8,128)(2,1)}, bf16[4096,512]{1,0:T(8,128)(2,1)}) async-done(((bf16[4096,512]{1,0:T(8,128)(2,1)}, bf16[4096,512]{1,0:T(8,128)(2,1)}), (bf16[4096,512]{1,0:T(8,128)(2,1)}, bf16[4096,512]{1,0:T(8,128)(2,1)})) %all-reduce.3.cloned.1.call-update) | async-done | bytes 8388624 | tf_op jit(solution)/shard_map/psum | solution.py:20
  298.3 10.5 %multiply_add_fusion = f32[512,1024]{1,0:T(8,128)} fusion(f32[512,1024]{1,0:T(8,128)S(1)} %copy-done.2, bf16[4096,512]{1,0:T(8,128)(2,1)} %all-gather.3.cloned.1.call-done, bf16[4096,512]{1,0:T(8,128)(2,1)} %get-tuple-element.5, bf16[4096,512]{1,0:T(8,128)(2,1)} %get-tuple-element.6), kind=kOutput, calls=%fused_computation.12 | convolution fusion | flops 4313317376 | bytes 16777216 | tf_op jit(solution)/shard_map/dot_general | solution.py:72
  308.9 56.4 %reduce-scatter.2.cloned.1.call-done = bf16[512,256]{1,0:T(8,128)(2,1)} async-done(((bf16[512,4096]{1,0:T(8,128)(2,1)}), bf16[512,256]{1,0:T(8,128)(2,1)}) %reduce-scatter.2.cloned.1.call-update) | async-done | bytes 262160 | tf_op jit(solution)/shard_map/reduce_scatter | solution.py:64
  365.3 1.8 multiply_add_fusion.1
  367.1 55.3 %all-gather.5.cloned.1.call-done = bf16[512,8192]{0,1:T(8,128)(2,1)} async-done(((bf16[512,512]{0,1:T(8,128)(2,1)}), bf16[512,8192]{0,1:T(8,128)(2,1)}) %all-gather.5.cloned.1.call-update) | async-done | bytes 8388624 | tf_op jit(solution)/shard_map/all_gather | solution.py:80
  422.5 11.1 %convolution_convert_fusion = bf16[512,512]{1,0:T(8,128)(2,1)} fusion(bf16[512,8192]{0,1:T(8,128)(2,1)} %all-gather.5.cloned.1.call-done, bf16[512,8192]{1,0:T(8,128)(2,1)} %param.11), kind=kOutput, calls=%fused_computation.19 | convolution fusion | flops 4295229440 | bytes 17301504 | tf_op jit(solution)/shard_map/dot_general | solution.py:79
  (31 shorter events, 10.4 us)
Async XLA Ops:
  32.2 23.7 %all-to-all-start = ((bf16[64,16,512]{2,0,1:T(8,128)(2,1)}), bf16[64,16,512]{2,0,1:T(8,128)(2,1)S(1)}, u32[]{:S(2)}, u32[]{:S(2)}) async-start(bf16[64,16,512]{2,0,1:T(8,128)(2,1)} %copy.13), calls=%async_computation | async-start | bytes 2097152 | tf_op jit(solution)/shard_map/all_to_all | solution.py:39
  40.0 89.7 %all-gather.3.cloned.1.call-start = ((), (), s32[]{:S(2)}) async-start(), calls=%async_computation.2 | async-start | bytes 4718592 | tf_op jit(solution)/shard_map/all_gather | solution.py:42
  58.8 239.5 %all-reduce.3.cloned.1.call-start = ((), (), s32[]{:S(2)}) async-start(), calls=%async_computation.5 | async-start | bytes 16777216 | tf_op jit(solution)/shard_map/psum | solution.py:20
  135.7 1.0 copy-start
  135.8 229.5 %reduce-scatter.2.cloned.1.call-start = ((), (), s32[]{:S(2)}) async-start(), calls=%async_computation.3 | async-start | bytes 4456448 | tf_op jit(solution)/shard_map/reduce_scatter | solution.py:64
  147.1 16.5 %collective-permute-start = (bf16[512,512]{1,0:T(8,128)(2,1)}, bf16[512,512]{1,0:T(8,128)(2,1)S(1)}, u32[]{:S(2)}, u32[]{:S(2)}) collective-permute-start(bf16[512,512]{1,0:T(8,128)(2,1)} %get-tuple-element.11), channel_id=1, source_target_pairs={{80,0},{96,16},{112,32},{0,48},{16,64},{32,80},{48,96},{64,112},{8... | collective-permute-start | bytes 1572872 | tf_op jit(solution)/shard_map/ppermute | solution.py:15
  147.1 25.1 %collective-permute-start.1 = (bf16[512,512]{1,0:T(8,128)(2,1)}, bf16[512,512]{1,0:T(8,128)(2,1)}, u32[]{:S(2)}, u32[]{:S(2)}) collective-permute-start(bf16[512,512]{1,0:T(8,128)(2,1)} %get-tuple-element.10), channel_id=1, source_target_pairs={{96,0},{112,16},{0,32},{16,48},{32,64},{48,80},{64,96},{80,112},{9... | collective-permute-start | bytes 1572872 | tf_op jit(solution)/shard_map/ppermute | solution.py:15
  147.9 39.7 %collective-permute-start.2 = (bf16[512,512]{1,0:T(8,128)(2,1)}, bf16[512,512]{1,0:T(8,128)(2,1)S(1)}, u32[]{:S(2)}, u32[]{:S(2)}) collective-permute-start(bf16[512,512]{1,0:T(8,128)(2,1)} %get-tuple-element.9), channel_id=1, source_target_pairs={{112,0},{0,16},{16,32},{32,48},{48,64},{64,80},{80,96},{96,112},{1... | collective-permute-start | bytes 1572872 | tf_op jit(solution)/shard_map/ppermute | solution.py:15
  198.6 99.8 %copy-start.2 = (f32[512,1024]{1,0:T(8,128)S(1)}, f32[512,1024]{1,0:T(8,128)}, u32[]{:S(2)}) copy-start(f32[512,1024]{1,0:T(8,128)} %param.9) | copy-start | bytes 6291460
  198.6 223.9 %all-gather.5.cloned.1.call-start = ((), (), s32[]{:S(2)}) async-start(), calls=%async_computation.4 | async-start | bytes 8912896 | tf_op jit(solution)/shard_map/all_gather | solution.py:80
  298.3 67.0 %copy-start.1 = (f32[512,256]{1,0:T(8,128)S(1)}, f32[512,256]{1,0:T(8,128)}, u32[]{:S(2)}) copy-start(f32[512,256]{1,0:T(8,128)} %param.8) | copy-start | bytes 1572868
Sparse Core Ops, SparseCore 0:
  58.9 70.7 all-gather.2
  135.9 162.4 all-reduce.2
  300.7 64.4 reduce-scatter.1
  367.4 54.9 all-gather.4
where the time goes:
time: 441 us; the launch traced here: 440 us
  waiting for transfers between devices  323 us (73%)
  other arithmetic  40 us (9%)
  matrix products  33.6 us (8%)
  local copies, waits for them, and re-layouts  17.4 us (4%)
  between operations  13.9 us (3%)
  starting transfers between devices  12 us (3%)
    psum x1, waiting for transfers between devices, broadcast(): return lax.psum(block, axis)  92.8 us
    all_gather x1, waiting for transfers between devices, shards(): column_panel = lax.all_gather(grad_tile, 'row', axis=0, tiled=True)  70.9 us
    reduce_scatter x1, waiting for transfers between devices, shards(): lax.psum_scatter(left_part.astype(jnp.bfloat16), 'col', scatter_dimension...  56.4 us
    all_gather x1, waiting for transfers between devices, shards(): lax.all_gather(left_mixed, 'col', axis=1, tiled=True)  55.3 us
    ppermute x3, waiting for transfers between devices, shifted(): return lax.ppermute(block, axis, route)  33.6 us
    unnamed x6, other arithmetic  29.3 us
    all_to_all x1, waiting for transfers between devices, shards(): lax.all_to_all(held_rows, 'col', split_axis=1, concat_axis=0, tiled=True)  14 us
    dot_general x1, matrix products, shards(): lax.dot_general(lax.all_gather(left_mixed, 'col', axis=1, tiled=True), ri...  11.1 us
  transfers between devices with their start and end apart: 8, of which 8 were waited for; matrix products, arithmetic and copies ran while one was open for 10% of the time, Pallas kernels for 0%

commit v1 on v0

--- a/solution.py
+++ b/solution.py
@@ -3,6 +3,7 @@
 import jax.numpy as jnp
 from jax import lax
 from jax.sharding import PartitionSpec as P
+from jax.lax import all_gather
 
 HQ = 4096
 DIN = 8192
@@ -16,8 +17,12 @@
 
 
 def broadcast(block, axis, source):
+
+    def plan_the_matrix(s0, along_axis):
+        return jnp.sum(all_gather(s0, along_axis), 0)
+
     block = jnp.where(lax.axis_index(axis) == source, block, jnp.zeros_like(block))
-    return lax.psum(block, axis)
+    return plan_the_matrix(block, axis)
 
 
 def slot_index(row_counts, tile_rows, capacity):

time: 441 us -> 1010 us (2.29)
  waiting for transfers between devices: 323 us -> 846 us
  other arithmetic: 40 us -> 90.1 us
    all_gather x0 -> x2, waiting for transfers between devices: none -> 625 us  [plan_the_matrix(): return jnp.sum(all_gather(s0, along_axis), 0)]
    psum x1 -> x0, waiting for transfers between devices: 92.8 us -> none  [broadcast(): return lax.psum(block, axis)]
    reduce_sum x0 -> x2, other arithmetic: none -> 50.1 us  [plan_the_matrix(): return jnp.sum(all_gather(s0, along_axis), 0)]
  transfers between devices with their start and end apart: 8 -> 9, of which waited for: 8 -> 9; matrix products, arithmetic and copies ran while one was open for 10% -> 6% of each run, Pallas kernels for 0% -> 0%
where the time goes in v1:
time: 1010 us
  waiting for transfers between devices  846 us (84%)
  other arithmetic  90.1 us (9%)
  matrix products  33.5 us (3%)
  local copies, waits for them, and re-layouts  16.3 us (2%)
  between operations  13.9 us (1%)
  starting transfers between devices  12.1 us (1%)
    all_gather x2, waiting for transfers between devices, plan_the_matrix(): return jnp.sum(all_gather(s0, along_axis), 0)  625 us
    all_gather x1, waiting for transfers between devices, shards(): column_panel = lax.all_gather(grad_tile, 'row', axis=0, tiled=True)  70.9 us
    all_gather x1, waiting for transfers between devices, shards(): lax.all_gather(left_mixed, 'col', axis=1, tiled=True)  55.5 us
    reduce_sum x2, other arithmetic, plan_the_matrix(): return jnp.sum(all_gather(s0, along_axis), 0)  50.1 us
    reduce_scatter x1, waiting for transfers between devices, shards(): lax.psum_scatter(left_part.astype(jnp.bfloat16), 'col', scatter_dimension...  46.6 us
    ppermute x3, waiting for transfers between devices, shifted(): return lax.ppermute(block, axis, route)  33.6 us
    unnamed x6, other arithmetic  29.3 us
  transfers between devices with their start and end apart: 9, of which 9 were waited for; matrix products, arithmetic and copies ran while one was open for 6% of the time, Pallas kernels for 0%

profile of v1, /device:TPU:1, one launch (start us, length us, event | category | flops | bytes accessed | tf_op | source)
XLA Modules:
  0.0 1012.1 jit_solution(4132442626029043398)
XLA Ops:
  7.2 22.8 %reduce.2 = bf16[524288]{0:T(1024)(128)(2,1)S(1)} reduce(bf16[1,1,524288]{2,1,0:T(2,128)(2,1)} %param.6, bf16[]{:T(256)} %constant.94), dimensions={0,1}, to_apply=%param.6.reduce_sub_computation | reduce | bytes 2097154 | tf_op args[0]
  32.2 7.8 all-to-all-start
  41.8 14.0 %all-to-all-done = bf16[64,16,512]{2,0,1:T(8,128)(2,1)S(1)} async-done(((bf16[64,16,512]{2,0,1:T(8,128)(2,1)}), bf16[64,16,512]{2,0,1:T(8,128)(2,1)S(1)}, u32[]{:S(2)}, u32[]{:S(2)}) %all-to-all-start) | async-done | bytes 1048608 | tf_op jit(solution)/shard_map/all_to_all | solution.py:44
  55.9 2.0 gather_fusion
  58.9 70.9 %all-gather.7.cloned.1.call-done = bf16[4096,512]{1,0:T(8,128)(2,1)} async-done(((bf16[512,512]{1,0:T(8,128)(2,1)}), bf16[4096,512]{1,0:T(8,128)(2,1)}) %all-gather.7.cloned.1.call-update) | async-done | bytes 4194320 | tf_op jit(solution)/shard_map/all_gather | solution.py:47
  129.7 5.2 constant_dynamic-update-slice_fusion.1
  135.0 2.7 copy.14
  137.7 2.5 slice_bitcast_fusion
  141.0 3.0 collective-permute-start.2
  144.0 12.6 %collective-permute-done = bf16[512,512]{1,0:T(8,128)(2,1)S(1)} collective-permute-done((bf16[512,512]{1,0:T(8,128)(2,1)}, bf16[512,512]{1,0:T(8,128)(2,1)S(1)}, u32[]{:S(2)}, u32[]{:S(2)}) %collective-permute-start) | collective-permute-done | bytes 524320 | tf_op jit(solution)/shard_map/ppermute | solution.py:16
  157.6 7.7 collective-permute-done.1
  165.3 2.0 convert_dynamic-update-slice_fusion.2
  167.3 13.3 %collective-permute-done.2 = bf16[512,512]{1,0:T(8,128)(2,1)S(1)} collective-permute-done((bf16[512,512]{1,0:T(8,128)(2,1)}, bf16[512,512]{1,0:T(8,128)(2,1)S(1)}, u32[]{:S(2)}, u32[]{:S(2)}) %collective-permute-start.2) | collective-permute-done | bytes 524320 | tf_op jit(solution)/shard_map/ppermute | solution.py:16
  186.7 4.6 dynamic-slice_convert_fusion
  191.6 6.6 fusion.9
  198.3 6.0 broadcast_select_fusion.1
  204.9 46.6 %reduce-scatter.2.cloned.1.call-done = bf16[512,256]{1,0:T(8,128)(2,1)} async-done(((bf16[512,4096]{1,0:T(8,128)(2,1)}), bf16[512,256]{1,0:T(8,128)(2,1)}) %reduce-scatter.2.cloned.1.call-update) | async-done | bytes 262160 | tf_op jit(solution)/shard_map/reduce_scatter | solution.py:69
  253.3 55.5 %all-gather.9.cloned.1.call-done = bf16[512,8192]{0,1:T(8,128)(2,1)} async-done(((bf16[512,512]{0,1:T(8,128)(2,1)}), bf16[512,8192]{0,1:T(8,128)(2,1)}) %all-gather.9.cloned.1.call-update) | async-done | bytes 8388624 | tf_op jit(solution)/shard_map/all_gather | solution.py:85
  308.8 11.1 %convolution_convert_fusion = bf16[512,512]{1,0:T(8,128)(2,1)} fusion(bf16[512,8192]{0,1:T(8,128)(2,1)} %all-gather.9.cloned.1.call-done, bf16[512,8192]{1,0:T(8,128)(2,1)} %param.11), kind=kOutput, calls=%fused_computation.19 | convolution fusion | flops 4295229440 | bytes 17301504 | tf_op jit(solution)/shard_map/dot_general | solution.py:84
  319.9 320.2 %all-gather.11.cloned.1.call-done = bf16[65536,512]{1,0:T(8,128)(2,1)} async-done(((bf16[4096,512]{1,0:T(8,128)(2,1)}), bf16[65536,512]{1,0:T(8,128)(2,1)}) %all-gather.11.cloned.1.call-update) | async-done | bytes 67108880 | tf_op jit(solution)/shard_map/all_gather | solution.py:22
  640.1 26.4 %reduce_sum.34 = bf16[4096,512]{1,0:T(8,128)(2,1)} reduce(bf16[16,4096,512]{2,1,0:T(8,128)(2,1)} %bitcast.9, bf16[]{:T(256)} %constant.90.clone.1), dimensions={0}, to_apply=%region_4.5 | reduce | flops 31457280 | bytes 71303168 | tf_op jit(solution)/shard_map/reduce_sum | solution.py:22
  666.4 304.9 %all-gather.13.cloned.1.call-done = bf16[65536,512]{1,0:T(8,128)(2,1)} async-done(((bf16[4096,512]{1,0:T(8,128)(2,1)}), bf16[65536,512]{1,0:T(8,128)(2,1)}) %all-gather.13.cloned.1.call-update) | async-done | bytes 67108880 | tf_op jit(solution)/shard_map/all_gather | solution.py:22
  971.3 23.7 %reduce_sum.35 = bf16[4096,512]{1,0:T(8,128)(2,1)} reduce(bf16[16,4096,512]{2,1,0:T(8,128)(2,1)} %bitcast.10, bf16[]{:T(256)} %constant.90.clone.1), dimensions={0}, to_apply=%region_5.6 | reduce | flops 31457280 | bytes 71303168 | tf_op jit(solution)/shard_map/reduce_sum | solution.py:22
  995.1 10.5 %multiply_add_fusion = f32[512,1024]{1,0:T(8,128)} fusion(f32[512,1024]{1,0:T(8,128)S(1)} %copy-done.1, bf16[4096,512]{1,0:T(8,128)(2,1)} %all-gather.7.cloned.1.call-done, bf16[4096,512]{1,0:T(8,128)(2,1)} %reduce_sum.35, bf16[4096,512]{1,0:T(8,128)(2,1)} %reduce_sum.34), kind=kOutput, calls=%fused_computation.12 | convolution fusion | flops 4313317376 | bytes 16777216 | tf_op jit(solution)/shard_map/dot_general | solution.py:77
  (34 shorter events, 15.5 us)
Async XLA Ops:
  32.2 23.7 %all-to-all-start = ((bf16[64,16,512]{2,0,1:T(8,128)(2,1)}), bf16[64,16,512]{2,0,1:T(8,128)(2,1)S(1)}, u32[]{:S(2)}, u32[]{:S(2)}) async-start(bf16[64,16,512]{2,0,1:T(8,128)(2,1)} %copy.13), calls=%async_computation | async-start | bytes 2097152 | tf_op jit(solution)/shard_map/all_to_all | solution.py:44
  40.0 89.7 %all-gather.7.cloned.1.call-start = ((), (), s32[]{:S(2)}) async-start(), calls=%async_computation.2 | async-start | bytes 4718592 | tf_op jit(solution)/shard_map/all_gather | solution.py:47
  58.8 192.7 %reduce-scatter.2.cloned.1.call-start = ((), (), s32[]{:S(2)}) async-start(), calls=%async_computation.3 | async-start | bytes 4456448 | tf_op jit(solution)/shard_map/reduce_scatter | solution.py:69
  140.2 16.5 %collective-permute-start = (bf16[512,512]{1,0:T(8,128)(2,1)}, bf16[512,512]{1,0:T(8,128)(2,1)S(1)}, u32[]{:S(2)}, u32[]{:S(2)}) collective-permute-start(bf16[512,512]{1,0:T(8,128)(2,1)} %get-tuple-element.9), channel_id=1, source_target_pairs={{80,0},{96,16},{112,32},{0,48},{16,64},{32,80},{48,96},{64,112},{8... | collective-permute-start | bytes 1572872 | tf_op jit(solution)/shard_map/ppermute | solution.py:16
  140.2 25.1 %collective-permute-start.1 = (bf16[512,512]{1,0:T(8,128)(2,1)}, bf16[512,512]{1,0:T(8,128)(2,1)}, u32[]{:S(2)}, u32[]{:S(2)}) collective-permute-start(bf16[512,512]{1,0:T(8,128)(2,1)} %get-tuple-element.8), channel_id=1, source_target_pairs={{96,0},{112,16},{0,32},{16,48},{32,64},{48,80},{64,96},{80,112},{9... | collective-permute-start | bytes 1572872 | tf_op jit(solution)/shard_map/ppermute | solution.py:16
  141.0 39.6 %collective-permute-start.2 = (bf16[512,512]{1,0:T(8,128)(2,1)}, bf16[512,512]{1,0:T(8,128)(2,1)S(1)}, u32[]{:S(2)}, u32[]{:S(2)}) collective-permute-start(bf16[512,512]{1,0:T(8,128)(2,1)} %get-tuple-element.7), channel_id=1, source_target_pairs={{112,0},{0,16},{16,32},{32,48},{48,64},{64,80},{80,96},{96,112},{1... | collective-permute-start | bytes 1572872 | tf_op jit(solution)/shard_map/ppermute | solution.py:16
  191.4 117.5 %all-gather.9.cloned.1.call-start = ((), (), s32[]{:S(2)}) async-start(), calls=%async_computation.4 | async-start | bytes 8912896 | tf_op jit(solution)/shard_map/all_gather | solution.py:85
  198.2 441.8 %all-gather.11.cloned.1.call-start = ((), (), s32[]{:S(2)}) async-start(), calls=%async_computation.5 | async-start | bytes 71303168 | tf_op jit(solution)/shard_map/all_gather | solution.py:22
  204.3 47.2 %copy-start = (f32[512,256]{1,0:T(8,128)S(1)}, f32[512,256]{1,0:T(8,128)}, u32[]{:S(2)}) copy-start(f32[512,256]{1,0:T(8,128)} %param.8) | copy-start | bytes 1572868
  204.3 767.0 %all-gather.13.cloned.1.call-start = ((), (), s32[]{:S(2)}) async-start(), calls=%async_computation.6 | async-start | bytes 71303168 | tf_op jit(solution)/shard_map/all_gather | solution.py:22
  971.3 23.7 %copy-start.1 = (f32[512,1024]{1,0:T(8,128)S(1)}, f32[512,1024]{1,0:T(8,128)}, u32[]{:S(2)}) copy-start(f32[512,1024]{1,0:T(8,128)} %param.9) | copy-start | bytes 6291460
Sparse Core Ops, SparseCore 0:
  58.9 70.7 all-gather.6
  191.5 59.9 reduce-scatter.1
  253.8 54.9 all-gather.8
  310.4 329.6 all-gather.10
  641.6 329.6 all-gather.12
